TPU v7x, 32 devices: a whole 2x2x4 slice. The times are simulated.
32 devices in a mesh: parts: 2 (over y), row: 2 (over x), col: 2 (over core), layer: 4 (over z).
Axes of the slice: x: 2, y: 2, z: 4, core: 2. Of those that a mesh axis runs over, the one named last changes fastest.
Arguments:
- dosages: bfloat16 [4096, 2048], P(('layer', 'col'), ('parts', 'row')), parts along dimension 1, may hold values from -6 to 6
- expression: bfloat16 [4096, 16384], P('layer', ('col', 'row')), may hold values from -6 to 6
Outputs:
- zscores: float32 [2048, 16384], P(('parts', 'row', 'layer'), 'col'), parts along dimension 0
There are 2 independent parts, one for each index of `parts`. A program takes and returns all parts, laid end to end along the dimension named above; an argument that names none is the same for every part. Nothing has to cross between parts.
All inputs are finite; a program needn't handle non-finite values.
Results may differ from a plain program's by a relative error of at most 0.0003.
Values may be sent and summed in bfloat16 or wider, within the bound.
No kernel may reach another device: no remote copies, remote signals or barrier semaphores. Data moves between devices by JAX's collectives and lax.ppermute only.
A program may use at most 128 MiB of HBM per device.

v0:
```python
import math

import jax
import jax.numpy as jnp
from jax import lax
from jax.sharding import PartitionSpec as P


def passed_along(value, axis, steps):
    count = lax.axis_size(axis)
    pairs = [(source, (source + steps) % count) for source in range(count)]
    return lax.ppermute(value, axis, pairs)


def contract(left_rows, right_rows):
    return lax.dot_general(
        left_rows, right_rows, (((0,), (0,)), ((), ())), preferred_element_type=jnp.float32
    )


def on_device(dosages, expression):
    factor = 1.0 / math.sqrt(dosages.shape[0] * lax.axis_size("col") * lax.axis_size("layer"))
    samples_all = lax.all_gather(dosages, "col", axis=0, tiled=True)
    width = expression.shape[1]
    count = lax.axis_size("row")
    my_index = lax.axis_index("row")

    def place(output, held, source):
        block = contract(samples_all, held) * factor
        return lax.dynamic_update_slice_in_dim(output, block, source * width, 1)

    output = jnp.zeros((dosages.shape[1], width * count), jnp.float32)
    output = place(output, expression, my_index)

    def advance(turn_index, carry):
        held, output = carry
        held = passed_along(held, "row", 1)
        source = (my_index - turn_index - 1) % count
        return (held, place(output, held, source))

    held, output = lax.fori_loop(0, count - 1, advance, (expression, output))
    return lax.psum_scatter(output, "layer", scatter_dimension=0, tiled=True)


def solution(mesh):
    return jax.shard_map(
        on_device,
        mesh=mesh,
        in_specs=(P(("layer", "col"), ("parts", "row")), P("layer", ("col", "row"))),
        out_specs=P(("parts", "row", "layer"), "col"),
        check_vma=False,
    )
```

profile of v0, /device:TPU:0, one launch (start us, length us, event | category | flops | bytes accessed | tf_op | source)
XLA Modules:
  0.0 489.4 jit_solution(3291303597821340126)
XLA Ops:
  6.5 0.0 all-gather.2.cloned.1.call-start
  6.5 3.0 collective-permute-start
  9.5 0.0 all-gather.2.cloned.1.call-update
  9.5 0.0 reduce-scatter.2.cloned.1.call-start
  9.6 11.1 %all-gather.2.cloned.1.call-done = bf16[1024,512]{1,0:T(8,128)(2,1)} async-done(((bf16[512,512]{1,0:T(8,128)(2,1)}), bf16[1024,512]{1,0:T(8,128)(2,1)}) %all-gather.2.cloned.1.call-update) | async-done | bytes 1048592 | tf_op jit(solution)/shard_map/all_gather | solution.py:23
  20.7 0.0 copy-start
  20.7 7.8 %broadcast_in_dim.3 = f32[512,8192]{1,0:T(8,128)} broadcast(f32[]{:T(128)} %constant.32.clone.1), dimensions={} | broadcast | bytes 16777220 | tf_op jit(solution)/shard_map/broadcast_in_dim | solution.py:32
  28.4 0.0 copy-done
  28.4 10.2 %multiply_dynamic-update-slice_fusion.1 = f32[512,8192]{1,0:T(8,128)} fusion(f32[512,8192]{1,0:T(8,128)} %broadcast_in_dim.3, s32[]{:T(128)S(6)} %select_n.16, bf16[1024,512]{1,0:T(8,128)(2,1)S(1)} %copy-done, bf16[1024,4096]{1,0:T(8,128)(2,1)} %param.3), kind=kOutput, calls=%fused_computation.1 | convolution fusion | flops 4297064448 | bytes 17825796 | tf_op jit(solution)/shard_map/dot_general | solution.py:16
  38.6 151.7 %collective-permute-done = bf16[1024,4096]{1,0:T(8,128)(2,1)} collective-permute-done((bf16[1024,4096]{1,0:T(8,128)(2,1)}, bf16[1024,4096]{1,0:T(8,128)(2,1)}, u32[]{:S(2)}, u32[]{:S(2)}) %collective-permute-start) | collective-permute-done | bytes 8388640 | tf_op jit(solution)/shard_map/while/body/eval_jaxpr/ppermute | solution.py:12
  190.3 10.2 %multiply_dynamic-update-slice_fusion = f32[512,8192]{1,0:T(8,128)} fusion(f32[512,8192]{1,0:T(8,128)} %multiply_dynamic-update-slice_fusion.1, s32[]{:T(128)S(6)} %select_n.18, bf16[1024,512]{1,0:T(8,128)(2,1)S(1)} %copy-done, bf16[1024,4096]{1,0:T(8,128)(2,1)} %collective-permute-done), kind=kOutput, calls=%fused_computation | convolution fusion | flops 4297064448 | bytes 17825796 | tf_op jit(solution)/shard_map/while/body/eval_jaxpr/dot_general | solution.py:16
  200.4 0.0 reduce-scatter.2.cloned.1.call-update
  200.5 282.1 %reduce-scatter.2.cloned.1.call-done = f32[128,8192]{1,0:T(8,128)} async-done(((f32[512,8192]{1,0:T(8,128)}), f32[128,8192]{1,0:T(8,128)}) %reduce-scatter.2.cloned.1.call-update) | async-done | bytes 4194320 | tf_op jit(solution)/shard_map/reduce_scatter | solution.py:42
Async XLA Ops:
  6.5 14.1 %all-gather.2.cloned.1.call-start = ((), (), s32[]{:S(2)}) async-start(), calls=%async_computation.1 | async-start | bytes 1572864 | tf_op jit(solution)/shard_map/all_gather | solution.py:23
  6.5 183.7 %collective-permute-start = (bf16[1024,4096]{1,0:T(8,128)(2,1)}, bf16[1024,4096]{1,0:T(8,128)(2,1)}, u32[]{:S(2)}, u32[]{:S(2)}) collective-permute-start(bf16[1024,4096]{1,0:T(8,128)(2,1)} %param.3), channel_id=1, source_target_pairs={{0,8},{8,0},{1,9},{9,1},{2,10},{10,2},{3,11},{11,3},{4,12},{12,4},... | collective-permute-start | bytes 25165832 | tf_op jit(solution)/shard_map/while/body/eval_jaxpr/ppermute | solution.py:12
  9.5 473.0 %reduce-scatter.2.cloned.1.call-start = ((), (), s32[]{:S(2)}) async-start(), calls=%async_computation.2 | async-start | bytes 20971520 | tf_op jit(solution)/shard_map/reduce_scatter | solution.py:42
  20.7 7.8 %copy-start = (bf16[1024,512]{1,0:T(8,128)(2,1)S(1)}, bf16[1024,512]{1,0:T(8,128)(2,1)}, u32[]{:S(2)}) copy-start(bf16[1024,512]{1,0:T(8,128)(2,1)} %all-gather.2.cloned.1.call-done) | copy-start | bytes 3145732
Sparse Core Ops, SparseCore 0:
  9.6 10.9 all-gather.1
  200.6 281.9 reduce-scatter.1
where the time goes:
time: 490 us; the launch traced here: 489 us
  waiting for transfers between devices  445 us (91%)
  matrix products  20.3 us (4%)
  between operations  13.4 us (3%)
  local copies, waits for them, and re-layouts  7.78 us (2%)
    reduce_scatter x1, waiting for transfers between devices, on_device(): return lax.psum_scatter(output, 'layer', scatter_dimension=0, tiled=True)  282 us
    ppermute x1, waiting for transfers between devices, passed_along(): return lax.ppermute(value, axis, pairs)  152 us
    dot_general x2, matrix products, contract(): lax.dot_general(left_rows, right_rows, (((0,), (0,)), ((), ())), preferre...  20.3 us
    all_gather x1, waiting for transfers between devices, on_device(): samples_all = lax.all_gather(dosages, 'col', axis=0, tiled=True)  11.1 us
  transfers between devices with their start and end apart: 3, of which 3 were waited for; matrix products, arithmetic and copies ran while one was open for 4% of the time, Pallas kernels for 0%

commit v1 on v0

v1 whole, which is shorter than its diff:
```python
import math

import jax
import jax.numpy as jnp
from jax import lax
from jax.sharding import PartitionSpec as P


def contract(left_rows, right_rows):
    return lax.dot_general(
        left_rows, right_rows, (((0,), (0,)), ((), ())), preferred_element_type=jnp.float32
    )


def full_dosages(local):
    samples = lax.all_gather(local, "col", axis=0, tiled=True)
    return lax.all_gather(samples, "row", axis=1, tiled=True)


def pick(d4, index):
    block = lax.dynamic_index_in_dim(d4, index, axis=2, keepdims=False)
    return block.reshape(block.shape[0], -1)


def on_device(dosages, expression):
    layers = lax.axis_size("layer")
    rows = lax.axis_size("row")
    layer = lax.axis_index("layer")
    row = lax.axis_index("row")
    factor = 1.0 / math.sqrt(dosages.shape[0] * lax.axis_size("col") * layers)

    samples, width = expression.shape
    block = dosages.shape[1] // layers
    half = layers // 2

    inward = [(0, 1), (layers - 1, layers - 2)]
    across = [(half - 1, half), (half, half - 1)]
    outward = [(1, 0), (layers - 2, layers - 1)]

    dosages_in = lax.ppermute(dosages, "layer", inward)
    own4 = full_dosages(dosages).reshape(samples, rows, layers, block)
    out4 = full_dosages(dosages_in).reshape(samples, rows, layers, block)

    is_left = layer < half
    outer = jnp.where(is_left, 0, layers - 1)
    near = layers - 1 - layer
    far = layers - 1 - outer

    own_far = jnp.concatenate([pick(own4, near), pick(own4, far)], axis=1)
    out_far = jnp.concatenate([pick(out4, near), pick(out4, far)], axis=1)
    own_here = pick(own4, layer)
    out_here = pick(out4, layer)
    own_outer = pick(own4, outer)
    stripe = rows * block

    chunks = max(1, min(8, width // 512))
    step = width // chunks

    output = jnp.zeros((block, rows * width), jnp.float32)
    for k in range(chunks):
        mine = expression[:, k * step:(k + 1) * step]
        theirs = lax.ppermute(mine, "layer", inward)
        sent = contract(own_far, mine) + contract(out_far, theirs)
        got = lax.ppermute(sent, "layer", across)
        to_outer = contract(own_outer, mine) + got[stripe:]
        from_inner = lax.ppermute(to_outer, "layer", outward)
        final = contract(own_here, mine) + contract(out_here, theirs) + got[:stripe] + from_inner
        final = (final * factor).reshape(rows, block, step)
        for shift in range(rows):
            target = (row + shift) % rows
            piece = lax.dynamic_index_in_dim(final, target, axis=0, keepdims=False)
            if shift:
                pairs = [(source, (source + shift) % rows) for source in range(rows)]
                piece = lax.ppermute(piece, "row", pairs)
            source = (row - shift) % rows
            output = lax.dynamic_update_slice_in_dim(output, piece, source * width + k * step, 1)
    return output


def solution(mesh):
    return jax.shard_map(
        on_device,
        mesh=mesh,
        in_specs=(P(("layer", "col"), ("parts", "row")), P("layer", ("col", "row"))),
        out_specs=P(("parts", "row", "layer"), "col"),
        check_vma=False,
    )
```

time: 490 us -> 400 us (0.82)
  waiting for transfers between devices: 445 us -> 294 us
  starting transfers between devices: 3.01 us -> 47.8 us
  matrix products: 20.3 us -> 29.8 us
  local copies, waits for them, and re-layouts: 7.78 us -> 13.4 us
    reduce_scatter x1 -> x0, waiting for transfers between devices: 282 us -> none  [on_device(): return lax.psum_scatter(output, 'layer', scatter_dimension=0, tiled=True)]
    ppermute x1 -> x33, waiting for transfers between devices: 152 us -> 231 us  [the longest x8 111 us: on_device(): from_inner = lax.ppermute(to_outer, 'layer', outward)]
    all_gather x1 -> x4, waiting for transfers between devices: 11.1 us -> 62.5 us  [the longest x2 53.1 us: full_dosages(): return lax.all_gather(samples, 'row', axis=1, tiled=True)]
    ppermute x1 -> x33, starting transfers between devices: 2.97 us -> 47.7 us  [the longest x8 17.1 us: on_device(): theirs = lax.ppermute(mine, 'layer', inward)]
    dot_general x2 -> x40, matrix products: 20.3 us -> 29.8 us  [contract(): lax.dot_general(left_rows, right_rows, (((0,), (0,)), ((), ())), preferre...]
    broadcast_in_dim x1, local copies, waits for them, and re-layouts: 7.77 us -> 0.4 us  [on_device(): output = jnp.zeros((block, rows * width), jnp.float32)]
    slice x0 -> x1, local copies, waits for them, and re-layouts: none -> 6.28 us  [on_device(): mine = expression[:, k * step:(k + 1) * step]]
  transfers between devices with their start and end apart: 3 -> 37, of which waited for: 3 -> 18; matrix products, arithmetic and copies ran while one was open for 4% -> 10% of each run, Pallas kernels for 0% -> 0%
where the time goes in v1:
time: 400 us; the launch traced here: 399 us
  waiting for transfers between devices  294 us (74%)
  starting transfers between devices  47.8 us (12%)
  matrix products  29.8 us (7%)
  between operations  14 us (4%)
  local copies, waits for them, and re-layouts  13.4 us (3%)
    ppermute x8, waiting for transfers between devices, on_device(): from_inner = lax.ppermute(to_outer, 'layer', outward)  111 us
    ppermute x8, waiting for transfers between devices, on_device(): theirs = lax.ppermute(mine, 'layer', inward)  90.4 us
    all_gather x2, waiting for transfers between devices, full_dosages(): return lax.all_gather(samples, 'row', axis=1, tiled=True)  53.1 us
    dot_general x40, matrix products, contract(): lax.dot_general(left_rows, right_rows, (((0,), (0,)), ((), ())), preferre...  29.8 us
    ppermute x8, waiting for transfers between devices, on_device(): piece = lax.ppermute(piece, 'row', pairs)  17.4 us
    ppermute x8, starting transfers between devices, on_device(): theirs = lax.ppermute(mine, 'layer', inward)  17.1 us
    ppermute x1, waiting for transfers between devices, on_device(): dosages_in = lax.ppermute(dosages, 'layer', inward)  11.4 us
    ppermute x8, starting transfers between devices, on_device(): from_inner = lax.ppermute(to_outer, 'layer', outward)  10.3 us
  transfers between devices with their start and end apart: 37, of which 18 were waited for; matrix products, arithmetic and copies ran while one was open for 10% of the time, Pallas kernels for 0%

profile of v1, /device:TPU:0, one launch (start us, length us, event | category | flops | bytes accessed | tf_op | source)
XLA Modules:
  0.0 399.0 jit_solution(11919725374042339640)
XLA Ops:
  6.5 2.0 copy.3
  8.7 5.0 %collective-permute-start = (bf16[512,512]{0,1:T(8,128)(2,1)}, bf16[512,512]{0,1:T(8,128)(2,1)S(1)}, u32[]{:S(2)}, u32[]{:S(2)}) collective-permute-start(bf16[512,512]{0,1:T(8,128)(2,1)} %copy.3), channel_id=1, source_target_pairs={{0,1},{3,2},{4,5},{7,6},{8,9},{11,10},{12,13},{15,14},{16,17},{19,... | collective-permute-start | bytes 1572872 | tf_op jit(solution)/shard_map/ppermute | solution.py:40
  13.7 11.4 %collective-permute-done = bf16[512,512]{0,1:T(8,128)(2,1)S(1)} collective-permute-done((bf16[512,512]{0,1:T(8,128)(2,1)}, bf16[512,512]{0,1:T(8,128)(2,1)S(1)}, u32[]{:S(2)}, u32[]{:S(2)}) %collective-permute-start) | collective-permute-done | bytes 524320 | tf_op jit(solution)/shard_map/ppermute | solution.py:40
  26.7 9.4 %all-gather.9.cloned.1.call-done = bf16[1024,512]{0,1:T(8,128)(2,1)} async-done(((bf16[512,512]{0,1:T(8,128)(2,1)}), bf16[1024,512]{0,1:T(8,128)(2,1)}) %all-gather.9.cloned.1.call-update) | async-done | bytes 1048592 | tf_op jit(solution)/shard_map/all_gather | solution.py:16
  36.2 6.3 %fusion.88 = (bf16[1024,512]{1,0:T(8,128)(2,1)}, bf16[1024,512]{1,0:T(8,128)(2,1)}, bf16[1024,512]{1,0:T(8,128)(2,1)}, bf16[1024,512]{1,0:T(8,128)(2,1)}, bf16[1...) fusion(bf16[1024,4096]{1,0:T(8,128)(2,1)} %param.3), kind=kLoop, calls=%fused_computation.129 | loop fusion | bytes 16777216 | tf_op jit(solution)/shard_map/slice | solution.py:61
  42.4 3.7 collective-permute-start.21
  46.2 1.4 collective-permute-start.17
  47.5 2.3 collective-permute-start.13
  49.8 1.3 collective-permute-start.9
  51.1 2.3 collective-permute-start.5
  53.4 18.5 %all-gather.7.cloned.1.call-done = bf16[1024,1024]{0,1:T(8,128)(2,1)} async-done(((bf16[1024,512]{0,1:T(8,128)(2,1)}), bf16[1024,1024]{0,1:T(8,128)(2,1)}) %all-gather.7.cloned.1.call-update) | async-done | bytes 2097168 | tf_op jit(solution)/shard_map/all_gather | solution.py:17
  72.0 34.5 %all-gather.11.cloned.1.call-done = bf16[1024,1024]{0,1:T(8,128)(2,1)} async-done(((bf16[1024,512]{0,1:T(8,128)(2,1)}), bf16[1024,1024]{0,1:T(8,128)(2,1)}) %all-gather.11.cloned.1.call-update) | async-done | bytes 2097168 | tf_op jit(solution)/shard_map/all_gather | solution.py:17
  106.5 2.6 constant_dynamic-slice_fusion.5
  109.1 2.1 fusion.42
  111.2 1.9 fusion.50
  116.4 3.4 collective-permute-start.1
  120.6 1.4 collective-permute-start.25
  122.7 1.4 collective-permute-start.29
  124.1 1.9 convolution_add_fusion.4
  126.0 11.3 %collective-permute-done.9 = bf16[1024,512]{1,0:T(8,128)(2,1)S(1)} collective-permute-done((bf16[1024,512]{1,0:T(8,128)(2,1)}, bf16[1024,512]{1,0:T(8,128)(2,1)S(1)}, u32[]{:S(2)}, u32[]{:S(2)}) %collective-permute-start.9) | collective-permute-done | bytes 1048608 | tf_op jit(solution)/shard_map/ppermute | solution.py:62
  141.7 18.2 %collective-permute-done.5 = bf16[1024,512]{1,0:T(8,128)(2,1)} collective-permute-done((bf16[1024,512]{1,0:T(8,128)(2,1)}, bf16[1024,512]{1,0:T(8,128)(2,1)}, u32[]{:S(2)}, u32[]{:S(2)}) %collective-permute-start.5) | collective-permute-done | bytes 1048608 | tf_op jit(solution)/shard_map/ppermute | solution.py:62
  160.6 1.9 convolution_add_fusion.6
  162.5 19.7 %collective-permute-done.1 = bf16[1024,512]{1,0:T(8,128)(2,1)S(1)} collective-permute-done((bf16[1024,512]{1,0:T(8,128)(2,1)S(1)}, bf16[1024,512]{1,0:T(8,128)(2,1)S(1)}, u32[]{:S(2)}, u32[]{:S(2)}) %collective-permute-start.1) | collective-permute-done | bytes 1048608 | tf_op jit(solution)/shard_map/ppermute | solution.py:62
  183.6 21.0 %collective-permute-done.25 = bf16[1024,512]{1,0:T(8,128)(2,1)S(1)} collective-permute-done((bf16[1024,512]{1,0:T(8,128)(2,1)S(1)}, bf16[1024,512]{1,0:T(8,128)(2,1)S(1)}, u32[]{:S(2)}, u32[]{:S(2)}) %collective-permute-start.25) | collective-permute-done | bytes 1048608 | tf_op jit(solution)/shard_map/ppermute | solution.py:62
  206.3 20.2 %collective-permute-done.29 = bf16[1024,512]{1,0:T(8,128)(2,1)S(1)} collective-permute-done((bf16[1024,512]{1,0:T(8,128)(2,1)S(1)}, bf16[1024,512]{1,0:T(8,128)(2,1)S(1)}, u32[]{:S(2)}, u32[]{:S(2)}) %collective-permute-start.29) | collective-permute-done | bytes 1048608 | tf_op jit(solution)/shard_map/ppermute | solution.py:62
  233.3 1.3 collective-permute-start.23
  235.0 1.3 collective-permute-start.19
  236.8 1.3 collective-permute-start.15
  238.6 1.3 collective-permute-start.7
  240.3 1.3 collective-permute-start.3
  242.1 70.3 %collective-permute-done.7 = f32[256,512]{1,0:T(8,128)S(1)} collective-permute-done((f32[256,512]{1,0:T(8,128)S(1)}, f32[256,512]{1,0:T(8,128)S(1)}, u32[]{:S(2)}, u32[]{:S(2)}) %collective-permute-start.7) | collective-permute-done | bytes 524320 | tf_op jit(solution)/shard_map/ppermute | solution.py:66
  312.4 1.3 collective-permute-start.11
  313.7 1.7 fusion.21
  315.4 21.5 %collective-permute-done.3 = f32[256,512]{1,0:T(8,128)S(1)} collective-permute-done((f32[256,512]{1,0:T(8,128)S(1)}, f32[256,512]{1,0:T(8,128)S(1)}, u32[]{:S(2)}, u32[]{:S(2)}) %collective-permute-start.3) | collective-permute-done | bytes 524320 | tf_op jit(solution)/shard_map/ppermute | solution.py:66
  338.7 1.3 collective-permute-start.31
  340.0 1.7 fusion.17
  341.7 6.4 %collective-permute-done.11 = f32[256,512]{1,0:T(8,128)S(1)} collective-permute-done((f32[256,512]{1,0:T(8,128)S(1)}, f32[256,512]{1,0:T(8,128)S(1)}, u32[]{:S(2)}, u32[]{:S(2)}) %collective-permute-start.11) | collective-permute-done | bytes 524320 | tf_op jit(solution)/shard_map/ppermute | solution.py:66
  348.1 1.5 collective-permute-start.4
  351.3 1.5 collective-permute-start.12
  353.4 6.0 %collective-permute-done.27 = f32[256,512]{1,0:T(8,128)S(1)} collective-permute-done((f32[256,512]{1,0:T(8,128)S(1)}, f32[256,512]{1,0:T(8,128)S(1)}, u32[]{:S(2)}, u32[]{:S(2)}) %collective-permute-start.27) | collective-permute-done | bytes 524320 | tf_op jit(solution)/shard_map/ppermute | solution.py:66
  359.4 1.5 collective-permute-start.16
  361.3 7.3 %collective-permute-done.31 = f32[256,512]{1,0:T(8,128)S(1)} collective-permute-done((f32[256,512]{1,0:T(8,128)S(1)}, f32[256,512]{1,0:T(8,128)S(1)}, u32[]{:S(2)}, u32[]{:S(2)}) %collective-permute-start.31) | collective-permute-done | bytes 524320 | tf_op jit(solution)/shard_map/ppermute | solution.py:66
  368.6 1.5 collective-permute-start.20
  371.7 1.5 collective-permute-start.28
  374.1 3.6 collective-permute-done.20
  377.8 5.6 %collective-permute-done.24 = f32[128,512]{1,0:T(8,128)S(1)} collective-permute-done((f32[128,512]{1,0:T(8,128)S(1)}, f32[128,512]{1,0:T(8,128)S(1)}, u32[]{:S(2)}, u32[]{:S(2)}) %collective-permute-start.24) | collective-permute-done | bytes 262176 | tf_op jit(solution)/shard_map/ppermute | solution.py:74
  383.4 5.5 %collective-permute-done.28 = f32[128,512]{1,0:T(8,128)S(1)} collective-permute-done((f32[128,512]{1,0:T(8,128)S(1)}, f32[128,512]{1,0:T(8,128)S(1)}, u32[]{:S(2)}, u32[]{:S(2)}) %collective-permute-start.28) | collective-permute-done | bytes 262176 | tf_op jit(solution)/shard_map/ppermute | solution.py:74
  389.0 2.7 collective-permute-done.32
  (113 shorter events, 31.0 us)
Async XLA Ops:
  6.5 19.4 %all-gather.5.cloned.1.call-start = ((), (), s32[]{:S(2)}) async-start(), calls=%async_computation | async-start | bytes 1572864 | tf_op jit(solution)/shard_map/all_gather | solution.py:16
  8.6 27.5 %all-gather.9.cloned.1.call-start = ((), (), s32[]{:S(2)}) async-start(), calls=%async_computation.2 | async-start | bytes 1572864 | tf_op jit(solution)/shard_map/all_gather | solution.py:16
  8.7 16.4 %collective-permute-start = (bf16[512,512]{0,1:T(8,128)(2,1)}, bf16[512,512]{0,1:T(8,128)(2,1)S(1)}, u32[]{:S(2)}, u32[]{:S(2)}) collective-permute-start(bf16[512,512]{0,1:T(8,128)(2,1)} %copy.3), channel_id=1, source_target_pairs={{0,1},{3,2},{4,5},{7,6},{8,9},{11,10},{12,13},{15,14},{16,17},{19,... | collective-permute-start | bytes 1572872 | tf_op jit(solution)/shard_map/ppermute | solution.py:40
  25.1 0.8 copy-start.4
  25.9 46.1 %all-gather.7.cloned.1.call-start = ((), (), s32[]{:S(2)}) async-start(), calls=%async_computation.1 | async-start | bytes 3145728 | tf_op jit(solution)/shard_map/all_gather | solution.py:17
  26.6 79.9 %all-gather.11.cloned.1.call-start = ((), (), s32[]{:S(2)}) async-start(), calls=%async_computation.3 | async-start | bytes 3145728 | tf_op jit(solution)/shard_map/all_gather | solution.py:17
  42.4 73.9 %collective-permute-start.21 = (bf16[1024,512]{1,0:T(8,128)(2,1)}, bf16[1024,512]{1,0:T(8,128)(2,1)S(1)}, u32[]{:S(2)}, u32[]{:S(2)}) collective-permute-start(bf16[1024,512]{1,0:T(8,128)(2,1)} %get-tuple-element.6), channel_id=1, source_target_pairs={{0,1},{3,2},{4,5},{7,6},{8,9},{11,10},{12,13},{15,14},{16,17},{19,... | collective-permute-start | bytes 3145736 | tf_op jit(solution)/shard_map/ppermute | solution.py:62
  46.2 74.4 %collective-permute-start.17 = (bf16[1024,512]{1,0:T(8,128)(2,1)}, bf16[1024,512]{1,0:T(8,128)(2,1)S(1)}, u32[]{:S(2)}, u32[]{:S(2)}) collective-permute-start(bf16[1024,512]{1,0:T(8,128)(2,1)} %get-tuple-element.7), channel_id=1, source_target_pairs={{0,1},{3,2},{4,5},{7,6},{8,9},{11,10},{12,13},{15,14},{16,17},{19,... | collective-permute-start | bytes 3145736 | tf_op jit(solution)/shard_map/ppermute | solution.py:62
  47.5 75.2 %collective-permute-start.13 = (bf16[1024,512]{1,0:T(8,128)(2,1)}, bf16[1024,512]{1,0:T(8,128)(2,1)}, u32[]{:S(2)}, u32[]{:S(2)}) collective-permute-start(bf16[1024,512]{1,0:T(8,128)(2,1)} %get-tuple-element.8), channel_id=1, source_target_pairs={{0,1},{3,2},{4,5},{7,6},{8,9},{11,10},{12,13},{15,14},{16,17},{19,... | collective-permute-start | bytes 3145736 | tf_op jit(solution)/shard_map/ppermute | solution.py:62
  49.8 87.6 %collective-permute-start.9 = (bf16[1024,512]{1,0:T(8,128)(2,1)}, bf16[1024,512]{1,0:T(8,128)(2,1)S(1)}, u32[]{:S(2)}, u32[]{:S(2)}) collective-permute-start(bf16[1024,512]{1,0:T(8,128)(2,1)} %get-tuple-element.9), channel_id=1, source_target_pairs={{0,1},{3,2},{4,5},{7,6},{8,9},{11,10},{12,13},{15,14},{16,17},{19,... | collective-permute-start | bytes 3145736 | tf_op jit(solution)/shard_map/ppermute | solution.py:62
  51.1 108.7 %collective-permute-start.5 = (bf16[1024,512]{1,0:T(8,128)(2,1)}, bf16[1024,512]{1,0:T(8,128)(2,1)}, u32[]{:S(2)}, u32[]{:S(2)}) collective-permute-start(bf16[1024,512]{1,0:T(8,128)(2,1)} %get-tuple-element.10), channel_id=1, source_target_pairs={{0,1},{3,2},{4,5},{7,6},{8,9},{11,10},{12,13},{15,14},{16,17},{19,... | collective-permute-start | bytes 3145736 | tf_op jit(solution)/shard_map/ppermute | solution.py:62
  106.5 6.6 %slice-start = ((s8[8388608]{0:T(1024)(128)(4,1)}), s8[4194304]{0:T(1024)(128)(4,1)S(1)}, s32[]{:S(2)}) async-start(s8[8388608]{0:T(1024)(128)(4,1)} %bitcast.105), calls=%async_computation.4 | async-start | bytes 8388608
  109.1 4.1 %slice-start.1 = ((s8[8388608]{0:T(1024)(128)(4,1)}), s8[4194304]{0:T(1024)(128)(4,1)S(1)}, s32[]{:S(2)}) async-start(s8[8388608]{0:T(1024)(128)(4,1)} %bitcast.105), calls=%async_computation.5 | async-start | bytes 8388608
  114.8 1.6 copy-start.3
  115.9 4.7 %copy-start.2 = (bf16[1024,512]{1,0:T(8,128)(2,1)S(1)}, bf16[1024,512]{1,0:T(8,128)(2,1)}, u32[]{:S(2)}) copy-start(bf16[1024,512]{1,0:T(8,128)(2,1)} %get-tuple-element.12) | copy-start | bytes 3145732
  116.4 65.8 %collective-permute-start.1 = (bf16[1024,512]{1,0:T(8,128)(2,1)S(1)}, bf16[1024,512]{1,0:T(8,128)(2,1)S(1)}, u32[]{:S(2)}, u32[]{:S(2)}) collective-permute-start(bf16[1024,512]{1,0:T(8,128)(2,1)S(1)} %copy-done.3), channel_id=1, source_target_pairs={{0,1},{3,2},{4,5},{7,6},{8,9},{11,10},{12,13},{15,14},{16,17},{19,... | collective-permute-start | bytes 3145736 | tf_op jit(solution)/shard_map/ppermute | solution.py:62
  119.8 2.9 copy-start.1
  120.6 84.1 %collective-permute-start.25 = (bf16[1024,512]{1,0:T(8,128)(2,1)S(1)}, bf16[1024,512]{1,0:T(8,128)(2,1)S(1)}, u32[]{:S(2)}, u32[]{:S(2)}) collective-permute-start(bf16[1024,512]{1,0:T(8,128)(2,1)S(1)} %copy-done.2), channel_id=1, source_target_pairs={{0,1},{3,2},{4,5},{7,6},{8,9},{11,10},{12,13},{15,14},{16,17},{19,... | collective-permute-start | bytes 3145736 | tf_op jit(solution)/shard_map/ppermute | solution.py:62
  122.7 103.7 %collective-permute-start.29 = (bf16[1024,512]{1,0:T(8,128)(2,1)S(1)}, bf16[1024,512]{1,0:T(8,128)(2,1)S(1)}, u32[]{:S(2)}, u32[]{:S(2)}) collective-permute-start(bf16[1024,512]{1,0:T(8,128)(2,1)S(1)} %copy-done.1), channel_id=1, source_target_pairs={{0,1},{3,2},{4,5},{7,6},{8,9},{11,10},{12,13},{15,14},{16,17},{19,... | collective-permute-start | bytes 3145736 | tf_op jit(solution)/shard_map/ppermute | solution.py:62
  137.4 92.3 %collective-permute-start.22 = (f32[512,512]{1,0:T(8,128)S(1)}, f32[512,512]{1,0:T(8,128)S(1)}, u32[]{:S(2)}, u32[]{:S(2)}) collective-permute-start(f32[512,512]{1,0:T(8,128)S(1)} %convolution_add_fusion.2), channel_id=1, source_target_pairs={{1,2},{2,1},{5,6},{6,5},{9,10},{10,9},{13,14},{14,13},{17,18},{18,... | collective-permute-start | bytes 3145736 | tf_op jit(solution)/shard_map/ppermute | solution.py:64
  159.8 71.1 %collective-permute-start.18 = (f32[512,512]{1,0:T(8,128)S(1)}, f32[512,512]{1,0:T(8,128)S(1)}, u32[]{:S(2)}, u32[]{:S(2)}) collective-permute-start(f32[512,512]{1,0:T(8,128)S(1)} %convolution_add_fusion.3), channel_id=1, source_target_pairs={{1,2},{2,1},{5,6},{6,5},{9,10},{10,9},{13,14},{14,13},{17,18},{18,... | collective-permute-start | bytes 3145736 | tf_op jit(solution)/shard_map/ppermute | solution.py:64
  182.2 49.9 %collective-permute-start.14 = (f32[512,512]{1,0:T(8,128)S(1)}, f32[512,512]{1,0:T(8,128)S(1)}, u32[]{:S(2)}, u32[]{:S(2)}) collective-permute-start(f32[512,512]{1,0:T(8,128)S(1)} %convolution_add_fusion.4), channel_id=1, source_target_pairs={{1,2},{2,1},{5,6},{6,5},{9,10},{10,9},{13,14},{14,13},{17,18},{18,... | collective-permute-start | bytes 3145736 | tf_op jit(solution)/shard_map/ppermute | solution.py:64
  204.7 28.6 %collective-permute-start.10 = (f32[512,512]{1,0:T(8,128)S(1)}, f32[512,512]{1,0:T(8,128)S(1)}, u32[]{:S(2)}, u32[]{:S(2)}) collective-permute-start(f32[512,512]{1,0:T(8,128)S(1)} %convolution_add_fusion.5), channel_id=1, source_target_pairs={{1,2},{2,1},{5,6},{6,5},{9,10},{10,9},{13,14},{14,13},{17,18},{18,... | collective-permute-start | bytes 3145736 | tf_op jit(solution)/shard_map/ppermute | solution.py:64
  226.5 8.6 %collective-permute-start.6 = (f32[512,512]{1,0:T(8,128)S(1)}, f32[512,512]{1,0:T(8,128)S(1)}, u32[]{:S(2)}, u32[]{:S(2)}) collective-permute-start(f32[512,512]{1,0:T(8,128)S(1)} %convolution_add_fusion.6), channel_id=1, source_target_pairs={{1,2},{2,1},{5,6},{6,5},{9,10},{10,9},{13,14},{14,13},{17,18},{18,... | collective-permute-start | bytes 3145736 | tf_op jit(solution)/shard_map/ppermute | solution.py:64
  229.7 7.1 %collective-permute-start.2 = (f32[512,512]{1,0:T(8,128)S(1)}, f32[512,512]{1,0:T(8,128)S(1)}, u32[]{:S(2)}, u32[]{:S(2)}) collective-permute-start(f32[512,512]{1,0:T(8,128)S(1)} %convolution_add_fusion.7), channel_id=1, source_target_pairs={{1,2},{2,1},{5,6},{6,5},{9,10},{10,9},{13,14},{14,13},{17,18},{18,... | collective-permute-start | bytes 3145736 | tf_op jit(solution)/shard_map/ppermute | solution.py:64
  230.9 7.7 %collective-permute-start.26 = (f32[512,512]{1,0:T(8,128)S(1)}, f32[512,512]{1,0:T(8,128)S(1)}, u32[]{:S(2)}, u32[]{:S(2)}) collective-permute-start(f32[512,512]{1,0:T(8,128)S(1)} %convolution_add_fusion.1), channel_id=1, source_target_pairs={{1,2},{2,1},{5,6},{6,5},{9,10},{10,9},{13,14},{14,13},{17,18},{18,... | collective-permute-start | bytes 3145736 | tf_op jit(solution)/shard_map/ppermute | solution.py:64
  232.1 8.2 %collective-permute-start.30 = (f32[512,512]{1,0:T(8,128)S(1)}, f32[512,512]{1,0:T(8,128)S(1)}, u32[]{:S(2)}, u32[]{:S(2)}) collective-permute-start(f32[512,512]{1,0:T(8,128)S(1)} %convolution_add_fusion), channel_id=1, source_target_pairs={{1,2},{2,1},{5,6},{6,5},{9,10},{10,9},{13,14},{14,13},{17,18},{18,... | collective-permute-start | bytes 3145736 | tf_op jit(solution)/shard_map/ppermute | solution.py:64
  233.3 116.9 %collective-permute-start.23 = (f32[256,512]{1,0:T(8,128)S(1)}, f32[256,512]{1,0:T(8,128)S(1)}, u32[]{:S(2)}, u32[]{:S(2)}) collective-permute-start(f32[256,512]{1,0:T(8,128)S(1)} %slice_add_fusion.2), channel_id=1, source_target_pairs={{1,0},{2,3},{5,4},{6,7},{9,8},{10,11},{13,12},{14,15},{17,16},{18,... | collective-permute-start | bytes 1572872 | tf_op jit(solution)/shard_map/ppermute | solution.py:66
  235.0 116.2 %collective-permute-start.19 = (f32[256,512]{1,0:T(8,128)S(1)}, f32[256,512]{1,0:T(8,128)S(1)}, u32[]{:S(2)}, u32[]{:S(2)}) collective-permute-start(f32[256,512]{1,0:T(8,128)S(1)} %slice_add_fusion.3), channel_id=1, source_target_pairs={{1,0},{2,3},{5,4},{6,7},{9,8},{10,11},{13,12},{14,15},{17,16},{18,... | collective-permute-start | bytes 1572872 | tf_op jit(solution)/shard_map/ppermute | solution.py:66
  236.8 101.9 %collective-permute-start.15 = (f32[256,512]{1,0:T(8,128)S(1)}, f32[256,512]{1,0:T(8,128)S(1)}, u32[]{:S(2)}, u32[]{:S(2)}) collective-permute-start(f32[256,512]{1,0:T(8,128)S(1)} %slice_add_fusion.4), channel_id=1, source_target_pairs={{1,0},{2,3},{5,4},{6,7},{9,8},{10,11},{13,12},{14,15},{17,16},{18,... | collective-permute-start | bytes 1572872 | tf_op jit(solution)/shard_map/ppermute | solution.py:66
  238.6 73.8 %collective-permute-start.7 = (f32[256,512]{1,0:T(8,128)S(1)}, f32[256,512]{1,0:T(8,128)S(1)}, u32[]{:S(2)}, u32[]{:S(2)}) collective-permute-start(f32[256,512]{1,0:T(8,128)S(1)} %slice_add_fusion.6), channel_id=1, source_target_pairs={{1,0},{2,3},{5,4},{6,7},{9,8},{10,11},{13,12},{14,15},{17,16},{18,... | collective-permute-start | bytes 1572872 | tf_op jit(solution)/shard_map/ppermute | solution.py:66
  240.3 96.6 %collective-permute-start.3 = (f32[256,512]{1,0:T(8,128)S(1)}, f32[256,512]{1,0:T(8,128)S(1)}, u32[]{:S(2)}, u32[]{:S(2)}) collective-permute-start(f32[256,512]{1,0:T(8,128)S(1)} %slice_add_fusion.7), channel_id=1, source_target_pairs={{1,0},{2,3},{5,4},{6,7},{9,8},{10,11},{13,12},{14,15},{17,16},{18,... | collective-permute-start | bytes 1572872 | tf_op jit(solution)/shard_map/ppermute | solution.py:66
  312.4 35.7 %collective-permute-start.11 = (f32[256,512]{1,0:T(8,128)S(1)}, f32[256,512]{1,0:T(8,128)S(1)}, u32[]{:S(2)}, u32[]{:S(2)}) collective-permute-start(f32[256,512]{1,0:T(8,128)S(1)} %slice_add_fusion.5), channel_id=1, source_target_pairs={{1,0},{2,3},{5,4},{6,7},{9,8},{10,11},{13,12},{14,15},{17,16},{18,... | collective-permute-start | bytes 1572872 | tf_op jit(solution)/shard_map/ppermute | solution.py:66
  336.9 22.5 %collective-permute-start.27 = (f32[256,512]{1,0:T(8,128)S(1)}, f32[256,512]{1,0:T(8,128)S(1)}, u32[]{:S(2)}, u32[]{:S(2)}) collective-permute-start(f32[256,512]{1,0:T(8,128)S(1)} %slice_add_fusion.1), channel_id=1, source_target_pairs={{1,0},{2,3},{5,4},{6,7},{9,8},{10,11},{13,12},{14,15},{17,16},{18,... | collective-permute-start | bytes 1572872 | tf_op jit(solution)/shard_map/ppermute | solution.py:66
  338.7 29.9 %collective-permute-start.31 = (f32[256,512]{1,0:T(8,128)S(1)}, f32[256,512]{1,0:T(8,128)S(1)}, u32[]{:S(2)}, u32[]{:S(2)}) collective-permute-start(f32[256,512]{1,0:T(8,128)S(1)} %slice_add_fusion), channel_id=1, source_target_pairs={{1,0},{2,3},{5,4},{6,7},{9,8},{10,11},{13,12},{14,15},{17,16},{18,... | collective-permute-start | bytes 1572872 | tf_op jit(solution)/shard_map/ppermute | solution.py:66
  348.1 22.9 %collective-permute-start.4 = (f32[128,512]{1,0:T(8,128)S(1)}, f32[128,512]{1,0:T(8,128)S(1)}, u32[]{:S(2)}, u32[]{:S(2)}) collective-permute-start(f32[128,512]{1,0:T(8,128)S(1)} %dynamic-slice_bitcast_fusion.7), channel_id=1, source_target_pairs={{0,8},{8,0},{1,9},{9,1},{2,10},{10,2},{3,11},{11,3},{4,12},{12,4},... | collective-permute-start | bytes 786440 | tf_op jit(solution)/shard_map/ppermute | solution.py:74
  350.2 21.6 %collective-permute-start.8 = (f32[128,512]{1,0:T(8,128)S(1)}, f32[128,512]{1,0:T(8,128)S(1)}, u32[]{:S(2)}, u32[]{:S(2)}) collective-permute-start(f32[128,512]{1,0:T(8,128)S(1)} %dynamic-slice_bitcast_fusion.6), channel_id=1, source_target_pairs={{0,8},{8,0},{1,9},{9,1},{2,10},{10,2},{3,11},{11,3},{4,12},{12,4},... | collective-permute-start | bytes 786440 | tf_op jit(solution)/shard_map/ppermute | solution.py:74
  351.3 22.1 %collective-permute-start.12 = (f32[128,512]{1,0:T(8,128)S(1)}, f32[128,512]{1,0:T(8,128)S(1)}, u32[]{:S(2)}, u32[]{:S(2)}) collective-permute-start(f32[128,512]{1,0:T(8,128)S(1)} %dynamic-slice_bitcast_fusion.5), channel_id=1, source_target_pairs={{0,8},{8,0},{1,9},{9,1},{2,10},{10,2},{3,11},{11,3},{4,12},{12,4},... | collective-permute-start | bytes 786440 | tf_op jit(solution)/shard_map/ppermute | solution.py:74
  359.4 14.7 %collective-permute-start.16 = (f32[128,512]{1,0:T(8,128)S(1)}, f32[128,512]{1,0:T(8,128)S(1)}, u32[]{:S(2)}, u32[]{:S(2)}) collective-permute-start(f32[128,512]{1,0:T(8,128)S(1)} %dynamic-slice_bitcast_fusion.4), channel_id=1, source_target_pairs={{0,8},{8,0},{1,9},{9,1},{2,10},{10,2},{3,11},{11,3},{4,12},{12,4},... | collective-permute-start | bytes 786440 | tf_op jit(solution)/shard_map/ppermute | solution.py:74
  368.6 9.2 %collective-permute-start.20 = (f32[128,512]{1,0:T(8,128)S(1)}, f32[128,512]{1,0:T(8,128)S(1)}, u32[]{:S(2)}, u32[]{:S(2)}) collective-permute-start(f32[128,512]{1,0:T(8,128)S(1)} %dynamic-slice_bitcast_fusion.3), channel_id=1, source_target_pairs={{0,8},{8,0},{1,9},{9,1},{2,10},{10,2},{3,11},{11,3},{4,12},{12,4},... | collective-permute-start | bytes 786440 | tf_op jit(solution)/shard_map/ppermute | solution.py:74
  371.1 12.3 %collective-permute-start.24 = (f32[128,512]{1,0:T(8,128)S(1)}, f32[128,512]{1,0:T(8,128)S(1)}, u32[]{:S(2)}, u32[]{:S(2)}) collective-permute-start(f32[128,512]{1,0:T(8,128)S(1)} %dynamic-slice_bitcast_fusion.2), channel_id=1, source_target_pairs={{0,8},{8,0},{1,9},{9,1},{2,10},{10,2},{3,11},{11,3},{4,12},{12,4},... | collective-permute-start | bytes 786440 | tf_op jit(solution)/shard_map/ppermute | solution.py:74
  371.7 17.2 %collective-permute-start.28 = (f32[128,512]{1,0:T(8,128)S(1)}, f32[128,512]{1,0:T(8,128)S(1)}, u32[]{:S(2)}, u32[]{:S(2)}) collective-permute-start(f32[128,512]{1,0:T(8,128)S(1)} %dynamic-slice_bitcast_fusion.1), channel_id=1, source_target_pairs={{0,8},{8,0},{1,9},{9,1},{2,10},{10,2},{3,11},{11,3},{4,12},{12,4},... | collective-permute-start | bytes 786440 | tf_op jit(solution)/shard_map/ppermute | solution.py:74
  373.4 18.4 %collective-permute-start.32 = (f32[128,512]{1,0:T(8,128)S(1)}, f32[128,512]{1,0:T(8,128)S(1)}, u32[]{:S(2)}, u32[]{:S(2)}) collective-permute-start(f32[128,512]{1,0:T(8,128)S(1)} %dynamic-slice_bitcast_fusion), channel_id=1, source_target_pairs={{0,8},{8,0},{1,9},{9,1},{2,10},{10,2},{3,11},{11,3},{4,12},{12,4},... | collective-permute-start | bytes 786440 | tf_op jit(solution)/shard_map/ppermute | solution.py:74
  389.0 2.7 copy-start
Sparse Core Ops, SparseCore 0:
  8.9 11.7 all-gather.4
  26.0 10.0 all-gather.8
  37.7 34.2 all-gather.6
  73.4 33.0 all-gather.10
